TPU v7x, 256 devices: a whole 4x4x8 slice. The times are simulated.
256 devices in a mesh: gx: 8 (over x, core), gy: 32 (over y, z).
Axes of the slice: x: 4, y: 4, z: 8, core: 2. Of those that a mesh axis runs over, the one named last changes fastest.
Arguments:
- hidden_in: bfloat16 [8192, 4096], P('gx', 'gy')
- norm_gain: bfloat16 [4096], P('gy'), may hold values from 0.099609375 to 1.8984375
- query_proj: bfloat16 [4096, 4096], P('gx', 'gy')
- kv_proj: bfloat16 [1024, 4096], P(None, 'gy')
- prompt_lengths: int32 [8], replicated, may hold values from 1 to 4096, 8192 in all
- cache_slot: int32 [512], replicated, may hold values from 0 to 511, as said below
Outputs:
- attention: bfloat16 [8192, 4096], P('gy', 'gx')
- kv_cache: bfloat16 [512, 16, 1024], P('gy', None, 'gx')
Inputs may be any that keep to these rules, and one draw needn't show every extreme that they name: `prompt_lengths`: the 8 prompts sum to 8192 tokens; the longest has exactly 4096. `cache_slot`: A permutation of the 512 slots; slot s is held by index s // 16 of gy. The 16 pages of one token block go to any one index at most 1 times, and every index receives exactly 16 pages.
All inputs are finite; a program needn't handle non-finite values.
Results may differ from a plain program's by a relative error of at most 0.0066.
The roundings to bfloat16 on the way count: a program that leaves them out, or rounds other values in their place, can miss the bound.
Values may be sent and summed in bfloat16 or wider, within the bound.
No kernel may reach another device: no remote copies, remote signals or barrier semaphores. Data moves between devices by JAX's collectives and lax.ppermute only.
A program may use at most 128 MiB of HBM per device.

v0:
```python
import math
import jax
import jax.numpy as jnp
from jax import lax
from jax.sharding import PartitionSpec as P

D = 4096
H = 32
KVH = 4
HD = 128
PAGES_DEV = 16
epsilon = 1e-06
rope_base = 5000000.0
masked_out = -1e30


def token_places(prompt_lengths, token_index):
    prompt_ends = jnp.cumsum(prompt_lengths)
    prompt_starts = prompt_ends - prompt_lengths
    segment = jnp.sum((token_index[:, None] >= prompt_ends[None, :]).astype(jnp.int32), axis=1)
    chosen = segment[:, None] == jnp.arange(prompt_lengths.shape[0], dtype=jnp.int32)[None, :]
    opening = jnp.sum(jnp.where(chosen, prompt_starts[None, :], 0), axis=1)
    return (segment, token_index - opening)


def rotate(vectors, places):
    half_size = vectors.shape[-1] // 2
    frequency = rope_base ** (-(jnp.arange(half_size, dtype=jnp.float32) * 2.0) / vectors.shape[-1])
    angles = places.astype(jnp.float32)[:, None] * frequency[None, :]
    cos_part = jnp.cos(angles)[:, None, :]
    sin_part = jnp.sin(angles)[:, None, :]
    leading = vectors[..., :half_size]
    trailing = vectors[..., half_size:]
    return jnp.concatenate(
        [leading * cos_part - trailing * sin_part, trailing * cos_part + leading * sin_part],
        axis=-1,
    )


def local(hidden_in, norm_gain, query_proj, kv_proj, prompt_lengths, cache_slot):
    count_gx = lax.axis_size("gx")
    count_gy = lax.axis_size("gy")
    where_gx = lax.axis_index("gx")
    where_gy = lax.axis_index("gy")
    local_rows = hidden_in.shape[0]
    block_tokens = local_rows * count_gx // count_gy
    all_tokens = block_tokens * count_gy
    heads_here = query_proj.shape[0] // HD
    group_size = H // KVH
    kv_head = where_gx * heads_here // group_size
    contract = (((1,), (1,)), ((), ()))
    kv_width = 2 * HD
    kv_start = kv_head * 2 * HD
    kv_rows = lax.dynamic_slice_in_dim(kv_proj, kv_start, kv_width, 0)
    widened = hidden_in.astype(jnp.float32)
    squares = jnp.sum(widened * widened, axis=1)
    totals = lax.psum(squares, "gy")
    normed = (
        widened * lax.rsqrt(totals / D + epsilon)[:, None] * norm_gain.astype(jnp.float32)[None, :]
    ).astype(jnp.bfloat16)
    gathered = lax.all_gather(normed, "gx", axis=0, tiled=True)
    stacked = jnp.concatenate([query_proj, kv_rows], axis=0)
    projected = lax.psum_scatter(
        lax.dot_general(gathered, stacked, contract, preferred_element_type=jnp.float32),
        "gy",
        scatter_dimension=0,
        tiled=True,
    )
    every_index = jnp.arange(all_tokens, dtype=jnp.int32)
    segment_all, place_all = token_places(prompt_lengths, every_index)
    first_query = where_gy * block_tokens
    token_index = first_query + jnp.arange(block_tokens, dtype=jnp.int32)
    segment_own = lax.dynamic_slice_in_dim(segment_all, first_query, block_tokens, 0)
    place_own = lax.dynamic_slice_in_dim(place_all, first_query, block_tokens, 0)
    query_cols = heads_here * HD
    queries = rotate(
        projected[:, :query_cols].reshape(block_tokens, heads_here, HD), place_own
    ).astype(jnp.bfloat16)
    keys = rotate(projected[:, query_cols : query_cols + HD][:, None, :], place_own)[
        :, 0, :
    ].astype(jnp.bfloat16)
    values = projected[:, query_cols + HD :].astype(jnp.bfloat16)
    cache_cols = jnp.where(where_gx % 2 == 0, keys, values)
    score_scale = 1.0 / math.sqrt(HD)
    last_query = first_query + block_tokens - 1
    first_segment = segment_own[0]
    initial = (
        jnp.full((heads_here, block_tokens), masked_out, jnp.float32),
        jnp.zeros((heads_here, block_tokens), jnp.float32),
        jnp.zeros((heads_here, block_tokens, HD), jnp.float32),
    )
    key_piece = lax.all_gather(keys, "gy", axis=0, tiled=True)
    value_piece = lax.all_gather(values, "gy", axis=0, tiled=True)
    block_count = key_piece.shape[0] // block_tokens
    key_blocks = key_piece.reshape(block_count, block_tokens, HD)
    value_blocks = value_piece.reshape(block_count, block_tokens, HD)

    def one_block(current, inputs):
        key_rows, value_rows, offset = inputs
        block_begin = offset * block_tokens
        key_segment = lax.dynamic_slice_in_dim(segment_all, block_begin, block_tokens, 0)
        skipped = jnp.logical_or(
            block_begin > last_query, key_segment[block_tokens - 1] < first_segment
        )

        def compute(previous):
            running_max, running_sum, running_acc = previous
            key_index = block_begin + jnp.arange(block_tokens, dtype=jnp.int32)
            allowed = (key_segment[None, :] == segment_own[:, None]) & (
                key_index[None, :] <= token_index[:, None]
            )
            scores = (
                jnp.einsum("qhd,kd->hqk", queries, key_rows, preferred_element_type=jnp.float32)
                * score_scale
            )
            scores = jnp.where(allowed[None], scores, masked_out)
            new_max = jnp.maximum(running_max, jnp.max(scores, axis=2))
            weights = jnp.where(allowed[None], jnp.exp(scores - new_max[..., None]), 0.0)
            factor = jnp.exp(running_max - new_max)
            new_sum = running_sum * factor + jnp.sum(weights, axis=2)
            update = jnp.einsum(
                "hqk,kd->hqd",
                weights.astype(jnp.bfloat16),
                value_rows,
                preferred_element_type=jnp.float32,
            )
            return (new_max, new_sum, running_acc * factor[..., None] + update)

        return (lax.cond(skipped, lambda previous: previous, compute, current), None)

    offsets = jnp.arange(block_count, dtype=jnp.int32)
    result, unused = lax.scan(one_block, initial, (key_blocks, value_blocks, offsets))
    final_max, final_sum, final_acc = result
    attention = (
        (final_acc / final_sum[..., None])
        .transpose(1, 0, 2)
        .reshape(block_tokens, query_cols)
        .astype(jnp.bfloat16)
    )
    pages_dev = PAGES_DEV
    page_len = block_tokens // pages_dev
    width_cols = cache_cols.shape[1]
    my_pages = cache_cols.reshape(pages_dev, page_len * width_cols)
    capacity = max(1, pages_dev // count_gy)
    slots_all = count_gy * capacity
    owners = (cache_slot // pages_dev).reshape(count_gy, pages_dev)
    page_range = jnp.arange(pages_dev, dtype=jnp.int32)
    earlier = page_range[None, :] < page_range[:, None]
    same_owner = owners[:, :, None] == owners[:, None, :]
    ranks = jnp.sum((same_owner & earlier[None]).astype(jnp.int32), axis=2)
    my_owner = lax.dynamic_index_in_dim(owners, where_gy, 0, keepdims=False)
    my_rank = lax.dynamic_index_in_dim(ranks, where_gy, 0, keepdims=False)
    target = my_owner * capacity + my_rank
    slot_range = jnp.arange(slots_all, dtype=jnp.int32)
    send_map = (slot_range[:, None] == target[None, :]).astype(jnp.bfloat16)
    outgoing = jnp.dot(send_map, my_pages, preferred_element_type=jnp.float32).astype(jnp.bfloat16)
    incoming = lax.all_to_all(outgoing, "gy", split_axis=0, concat_axis=0, tiled=True)
    wanted = where_gy * pages_dev + page_range
    matches = cache_slot[None, :] == wanted[:, None]
    page_ids = jnp.arange(cache_slot.shape[0], dtype=jnp.int32)
    source_page = jnp.sum(jnp.where(matches, page_ids[None, :], 0), axis=1)
    source_rank = jnp.sum(jnp.where(matches, ranks.reshape(-1)[None, :], 0), axis=1)
    source_slot = source_page // pages_dev * capacity + source_rank
    take_map = (source_slot[:, None] == slot_range[None, :]).astype(jnp.bfloat16)
    cache_block = jnp.dot(take_map, incoming, preferred_element_type=jnp.float32)
    cache_block = cache_block.astype(jnp.bfloat16).reshape(pages_dev, page_len, width_cols)
    return (attention, cache_block)


def solution(mesh):
    return jax.shard_map(
        local,
        mesh=mesh,
        in_specs=(P("gx", "gy"), P("gy"), P("gx", "gy"), P(None, "gy"), P(), P()),
        out_specs=(P("gy", "gx"), P("gy", None, "gx")),
        check_vma=False,
    )
```

profile of v0, /device:TPU:208, one launch (start us, length us, event | category | flops | bytes accessed | tf_op | source)
XLA Modules:
  0.0 692.0 jit_solution(10577667807313542377)
XLA Ops:
  8.4 58.9 %psum.7 = f32[1024]{0:T(1024)S(1)} all-reduce(f32[1024]{0:T(1024)S(1)} %fusion.19), channel_id=1, replica_groups=mesh['gx'=8,'gy'=32] {'gy'}, use_global_device_ids=true, to_apply=%region_1.2 | all-reduce | flops 1024 | bytes 8192 | tf_op jit(solution)/shard_map/psum | solution.py:57
  69.9 38.3 %all-gather.5.cloned.1.call-done = bf16[8192,128]{1,0:T(8,128)(2,1)} async-done(((bf16[1024,128]{1,0:T(8,128)(2,1)}), bf16[8192,128]{1,0:T(8,128)(2,1)}) %all-gather.5.cloned.1.call-update) | async-done | bytes 2097168 | tf_op jit(solution)/shard_map/all_gather | solution.py:61
  108.2 13.3 %fusion.23 = f32[8192,768]{0,1:T(8,128)} fusion(bf16[8192,128]{1,0:T(8,128)(2,1)} %all-gather.5.cloned.1.call-done, bf16[256,128]{1,0:T(8,128)(2,1)S(1)} %constant_dynamic-slice_fusion, bf16[512,128]{1,0:T(8,128)(2,1)} %param.12), kind=kOutput, calls=%fused_computation.42 | convolution fusion | flops 1611005952 | bytes 27459584 | tf_op jit(solution)/shard_map/dot_general | solution.py:64
  122.8 264.6 %reduce-scatter.2.cloned.1.call-done = f32[256,768]{0,1:T(8,128)} async-done(((f32[8192,768]{0,1:T(8,128)}), f32[256,768]{0,1:T(8,128)}) %reduce-scatter.2.cloned.1.call-update) | async-done | bytes 786448 | tf_op jit(solution)/shard_map/reduce_scatter | solution.py:63
  395.8 10.1 %all-to-all-start = ((bf16[32,2,1024]{2,1,0:T(2,128)(2,1)}), bf16[32,2,1024]{2,1,0:T(2,128)(2,1)S(1)}, u32[]{:S(2)}, u32[]{:S(2)}) async-start(bf16[32,2,1024]{2,1,0:T(2,128)(2,1)} %reshape.266), calls=%async_computation.1 | async-start | bytes 262144 | tf_op jit(solution)/shard_map/all_to_all | solution.py:157
  406.2 5.9 all-to-all-done
  413.1 52.7 %all-gather.7.cloned.1.call-done = bf16[8192,128]{0,1:T(8,128)(2,1)} async-done(((bf16[256,128]{0,1:T(8,128)(2,1)}), bf16[8192,128]{0,1:T(8,128)(2,1)}) %all-gather.7.cloned.1.call-update) | async-done | bytes 2097168 | tf_op jit(solution)/shard_map/all_gather | solution.py:93
  465.7 3.2 copy.72
  469.0 72.9 %all-gather.9.cloned.1.call-done = bf16[8192,1,128]{0,2,1:T(8,128)(2,1)} async-done(((bf16[256,1,128]{0,2,1:T(8,128)(2,1)}), bf16[8192,1,128]{0,2,1:T(8,128)(2,1)}) %all-gather.9.cloned.1.call-update) | async-done | bytes 2097168 | tf_op jit(solution)/shard_map/all_gather | solution.py:92
  541.8 4.1 copy.71
  546.0 138.6 %while.15 = (s32[]{:T(128)}, f32[4,256]{1,0:T(4,128)S(1)}, f32[4,256]{1,0:T(4,128)S(1)}, f32[4,256,128]{2,1,0:T(8,128)S(1)}, s32[32]{0:T(128)S(1)}, /*index=5*/s...) while((s32[]{:T(128)}, f32[4,256]{1,0:T(4,128)S(1)}, ...), condition=%wide.region_11.12_spmd.clone, body=%wide.region_6.11_spmd.clone.sunk | while | flops 137038352 | bytes 4926361 | solution.py:132
  568.6 2.1 conditional.3
  573.9 2.1 conditional.3
  584.5 2.1 conditional.3
  589.8 2.1 conditional.3
  595.1 2.1 conditional.3
  600.4 2.1 conditional.3
  605.7 2.1 conditional.3
  616.3 2.1 conditional.3
  626.9 2.1 conditional.3
  632.2 2.1 conditional.3
  637.5 2.1 conditional.3
  642.8 2.1 conditional.3
  648.1 2.1 conditional.3
  (377 shorter events, 99.4 us)
Async XLA Ops:
  7.2 62.7 %copy-start = (bf16[1024,128]{1,0:T(8,128)(2,1)S(1)}, bf16[1024,128]{1,0:T(8,128)(2,1)}, u32[]{:S(2)}) copy-start(bf16[1024,128]{1,0:T(8,128)(2,1)} %param.13) | copy-start | bytes 786436
  7.2 101.1 %all-gather.5.cloned.1.call-start = ((), (), s32[]{:S(2)}) async-start(), calls=%async_computation.2 | async-start | bytes 2359296 | tf_op jit(solution)/shard_map/all_gather | solution.py:61
  69.8 317.6 %reduce-scatter.2.cloned.1.call-start = ((), (), s32[]{:S(2)}) async-start(), calls=%async_computation.3 | async-start | bytes 25952256 | tf_op jit(solution)/shard_map/reduce_scatter | solution.py:63
  121.6 0.7 copy-start.2
  121.6 270.1 %copy-start.1 = (s32[512]{0:T(512)S(1)}, s32[512]{0:T(512)}, u32[]{:S(2)}) copy-start(s32[512]{0:T(512)} %param.15) | copy-start | bytes 6148
  121.6 344.1 %all-gather.7.cloned.1.call-start = ((), (), s32[]{:S(2)}) async-start(), calls=%async_computation.4 | async-start | bytes 2162688 | tf_op jit(solution)/shard_map/all_gather | solution.py:93
  387.5 5.6 slice-start
  390.3 151.5 %all-gather.9.cloned.1.call-start = ((), (), s32[]{:S(2)}) async-start(), calls=%async_computation.5 | async-start | bytes 2162688 | tf_op jit(solution)/shard_map/all_gather | solution.py:92
  395.8 16.3 %all-to-all-start = ((bf16[32,2,1024]{2,1,0:T(2,128)(2,1)}), bf16[32,2,1024]{2,1,0:T(2,128)(2,1)S(1)}, u32[]{:S(2)}, u32[]{:S(2)}) async-start(bf16[32,2,1024]{2,1,0:T(2,128)(2,1)} %reshape.266), calls=%async_computation.1 | async-start | bytes 262144 | tf_op jit(solution)/shard_map/all_to_all | solution.py:157
Sparse Core Ops, SparseCore 0:
  69.9 38.2 all-gather.4
  121.7 265.7 reduce-scatter.1
  390.5 75.2 all-gather.6
  468.1 73.7 all-gather.8
where the time goes:
time: 694 us; the launch traced here: 692 us
  waiting for transfers between devices  434 us (63%)
  loops' own time  63.5 us (9%)
  blocking collectives  58.9 us (8%)
  local copies, waits for them, and re-layouts  52.8 us (8%)
  matrix products  42.2 us (6%)
  other arithmetic  16 us (2%)
  between operations  14 us (2%)
  starting transfers between devices  10.3 us (1%)
    reduce_scatter x1, waiting for transfers between devices, local(): lax.psum_scatter(lax.dot_general(gathered, stacked, contract, preferred_e...  265 us
    all_gather x1, waiting for transfers between devices, local(): key_piece = lax.all_gather(keys, 'gy', axis=0, tiled=True)  72.9 us
    another operation x1, loops' own time, local(): lax.scan(one_block, initial, (key_blocks, value_blocks, offsets))  62.1 us
    psum x1, blocking collectives, local(): totals = lax.psum(squares, 'gy')  58.9 us
    all_gather x1, waiting for transfers between devices, local(): value_piece = lax.all_gather(values, 'gy', axis=0, tiled=True)  52.7 us
    all_gather x1, waiting for transfers between devices, local(): gathered = lax.all_gather(normed, 'gx', axis=0, tiled=True)  38.3 us
    dot_general x17, matrix products, compute(): jnp.einsum('qhd,kd->hqk', queries, key_rows, preferred_element_type=jnp.f...  19.9 us
    slice x32, local copies, waits for them, and re-layouts, one_block(): key_segment[block_tokens - 1] < first_segment  18.9 us
  transfers between devices with their start and end apart: 5, of which 5 were waited for; matrix products, arithmetic and copies ran while one was open for 1% of the time, Pallas kernels for 0%

commit v1 on v0

--- a/solution.py
+++ b/solution.py
@@ -1,8 +1,10 @@
+import functools
 import math
 import jax
 import jax.numpy as jnp
 from jax import lax
 from jax.sharding import PartitionSpec as P
+from jax.lax import all_to_all, axis_size
 
 D = 4096
 H = 32
@@ -12,6 +14,18 @@
 epsilon = 1e-06
 rope_base = 5000000.0
 masked_out = -1e30
+
+
+def make_the_row(piece_in, pos_dim):
+    return jnp.concatenate(
+        all_to_all(
+            jnp.stack([piece_in for _ in range(axis_size("gy"))]), "gy", split_axis=0, concat_axis=0
+        ),
+        axis=pos_dim,
+    )
+
+
+cover_bars = functools.partial(make_the_row, pos_dim=0)
 
 
 def token_places(prompt_lengths, token_index):
@@ -89,7 +103,7 @@
         jnp.zeros((heads_here, block_tokens), jnp.float32),
         jnp.zeros((heads_here, block_tokens, HD), jnp.float32),
     )
-    key_piece = lax.all_gather(keys, "gy", axis=0, tiled=True)
+    key_piece = cover_bars(keys)
     value_piece = lax.all_gather(values, "gy", axis=0, tiled=True)
     block_count = key_piece.shape[0] // block_tokens
     key_blocks = key_piece.reshape(block_count, block_tokens, HD)

time: 694 us -> 645 us (0.929)
  waiting for transfers between devices: 434 us -> 376 us
  starting transfers between devices: 10.3 us -> 19.4 us
    all_gather x1 -> x0, waiting for transfers between devices: 72.9 us -> none  [local(): key_piece = lax.all_gather(keys, 'gy', axis=0, tiled=True)]
    all_gather x1, waiting for transfers between devices: 52.7 us -> 68.2 us  [local(): value_piece = lax.all_gather(values, 'gy', axis=0, tiled=True)]
    all_to_all x0 -> x1, starting transfers between devices: none -> 9.18 us  [make_the_row(): all_to_all(jnp.stack([piece_in for _ in range(axis_size('gy'))]), 'gy', s...]
  transfers between devices with their start and end apart: 5 -> 5, of which waited for: 5 -> 4; matrix products, arithmetic and copies ran while one was open for 1% -> 1% of each run, Pallas kernels for 0% -> 0%
where the time goes in v1:
time: 645 us; the launch traced here: 642 us
  waiting for transfers between devices  376 us (58%)
  loops' own time  64.5 us (10%)
  blocking collectives  58.9 us (9%)
  local copies, waits for them, and re-layouts  51.6 us (8%)
  matrix products  42.2 us (7%)
  starting transfers between devices  19.4 us (3%)
  other arithmetic  15.4 us (2%)
  between operations  14 us (2%)
    reduce_scatter x1, waiting for transfers between devices, local(): lax.psum_scatter(lax.dot_general(gathered, stacked, contract, preferred_e...  264 us
    all_gather x1, waiting for transfers between devices, local(): value_piece = lax.all_gather(values, 'gy', axis=0, tiled=True)  68.2 us
    another operation x1, loops' own time, local(): lax.scan(one_block, initial, (key_blocks, value_blocks, offsets))  63.1 us
    psum x1, blocking collectives, local(): totals = lax.psum(squares, 'gy')  58.9 us
    all_gather x1, waiting for transfers between devices, local(): gathered = lax.all_gather(normed, 'gx', axis=0, tiled=True)  38.3 us
    dot_general x17, matrix products, compute(): jnp.einsum('qhd,kd->hqk', queries, key_rows, preferred_element_type=jnp.f...  19.9 us
    dynamic_slice x32, local copies, waits for them, and re-layouts, local(): lax.scan(one_block, initial, (key_blocks, value_blocks, offsets))  19.8 us
    slice x32, local copies, waits for them, and re-layouts, one_block(): key_segment[block_tokens - 1] < first_segment  18.9 us
  transfers between devices with their start and end apart: 5, of which 4 were waited for; matrix products, arithmetic and copies ran while one was open for 1% of the time, Pallas kernels for 0%

profile of v1, /device:TPU:208, one launch (start us, length us, event | category | flops | bytes accessed | tf_op | source)
XLA Modules:
  0.0 642.4 jit_solution(6042787409294771400)
XLA Ops:
  8.4 58.9 %psum.7 = f32[1024]{0:T(1024)S(1)} all-reduce(f32[1024]{0:T(1024)S(1)} %fusion.19), channel_id=1, replica_groups=mesh['gx'=8,'gy'=32] {'gy'}, use_global_device_ids=true, to_apply=%region_1.2 | all-reduce | flops 1024 | bytes 8192 | tf_op jit(solution)/shard_map/psum | solution.py:71
  69.9 38.3 %all-gather.3.cloned.1.call-done = bf16[8192,128]{1,0:T(8,128)(2,1)} async-done(((bf16[1024,128]{1,0:T(8,128)(2,1)}), bf16[8192,128]{1,0:T(8,128)(2,1)}) %all-gather.3.cloned.1.call-update) | async-done | bytes 2097168 | tf_op jit(solution)/shard_map/all_gather | solution.py:75
  108.2 13.3 %fusion.23 = f32[8192,768]{0,1:T(8,128)} fusion(bf16[8192,128]{1,0:T(8,128)(2,1)} %all-gather.3.cloned.1.call-done, bf16[256,128]{1,0:T(8,128)(2,1)S(1)} %constant_dynamic-slice_fusion, bf16[512,128]{1,0:T(8,128)(2,1)} %param.12), kind=kOutput, calls=%fused_computation.42 | convolution fusion | flops 1611005952 | bytes 27459584 | tf_op jit(solution)/shard_map/dot_general | solution.py:78
  123.3 264.1 %reduce-scatter.2.cloned.1.call-done = f32[256,768]{0,1:T(8,128)} async-done(((f32[8192,768]{0,1:T(8,128)}), f32[256,768]{0,1:T(8,128)}) %reduce-scatter.2.cloned.1.call-update) | async-done | bytes 786448 | tf_op jit(solution)/shard_map/reduce_scatter | solution.py:77
  392.5 10.1 %all-to-all-start.1 = ((bf16[32,2,1024]{2,1,0:T(2,128)(2,1)}), bf16[32,2,1024]{2,1,0:T(2,128)(2,1)S(1)}, u32[]{:S(2)}, u32[]{:S(2)}) async-start(bf16[32,2,1024]{2,1,0:T(2,128)(2,1)} %reshape.263), calls=%async_computation.2 | async-start | bytes 262144 | tf_op jit(solution)/shard_map/all_to_all | solution.py:171
  403.5 5.1 all-to-all-done.1
  410.4 9.2 %all-to-all-start = ((bf16[32,256,128]{2,1,0:T(8,128)(2,1)}), bf16[32,256,128]{2,1,0:T(8,128)(2,1)}, u32[]{:S(2)}, u32[]{:S(2)}) async-start(bf16[32,256,128]{2,1,0:T(8,128)(2,1)} %stack.2), calls=%async_computation.1 | async-start | bytes 4194304 | tf_op jit(solution)/shard_map/all_to_all | solution.py:21
  422.9 68.2 %all-gather.5.cloned.1.call-done = bf16[8192,128]{0,1:T(8,128)(2,1)} async-done(((bf16[256,128]{0,1:T(8,128)(2,1)}), bf16[8192,128]{0,1:T(8,128)(2,1)}) %all-gather.5.cloned.1.call-update) | async-done | bytes 2097168 | tf_op jit(solution)/shard_map/all_gather | solution.py:107
  491.1 3.2 copy.71
  494.4 140.6 %while.15 = (s32[]{:T(128)}, f32[4,256]{1,0:T(4,128)S(1)}, f32[4,256]{1,0:T(4,128)S(1)}, f32[4,256,128]{2,1,0:T(8,128)S(1)}, s32[32]{0:T(128)S(1)}, /*index=5*/s...) while((s32[]{:T(128)}, f32[4,256]{1,0:T(4,128)S(1)}, ...), condition=%wide.region_11.12_spmd.clone, body=%wide.region_6.11_spmd.clone.sunk | while | flops 137038352 | bytes 4926361 | solution.py:146
  517.4 2.1 conditional.3
  522.7 2.1 conditional.3
  528.1 2.1 conditional.3
  533.5 2.1 conditional.3
  538.8 2.1 conditional.3
  544.2 2.1 conditional.3
  549.6 2.1 conditional.3
  554.9 2.1 conditional.3
  560.3 2.1 conditional.3
  565.6 2.1 conditional.3
  571.0 2.1 conditional.3
  581.7 2.1 conditional.3
  592.5 2.1 conditional.3
  603.2 2.1 conditional.3
  (377 shorter events, 100.3 us)
Async XLA Ops:
  7.2 62.7 %copy-start = (bf16[1024,128]{1,0:T(8,128)(2,1)S(1)}, bf16[1024,128]{1,0:T(8,128)(2,1)}, u32[]{:S(2)}) copy-start(bf16[1024,128]{1,0:T(8,128)(2,1)} %param.13) | copy-start | bytes 786436
  7.2 101.1 %all-gather.3.cloned.1.call-start = ((), (), s32[]{:S(2)}) async-start(), calls=%async_computation.3 | async-start | bytes 2359296 | tf_op jit(solution)/shard_map/all_gather | solution.py:75
  69.8 317.6 %reduce-scatter.2.cloned.1.call-start = ((), (), s32[]{:S(2)}) async-start(), calls=%async_computation.4 | async-start | bytes 25952256 | tf_op jit(solution)/shard_map/reduce_scatter | solution.py:77
  121.6 0.7 copy-start.2
  121.6 0.8 copy-start.1
  392.5 16.1 %all-to-all-start.1 = ((bf16[32,2,1024]{2,1,0:T(2,128)(2,1)}), bf16[32,2,1024]{2,1,0:T(2,128)(2,1)S(1)}, u32[]{:S(2)}, u32[]{:S(2)}) async-start(bf16[32,2,1024]{2,1,0:T(2,128)(2,1)} %reshape.263), calls=%async_computation.2 | async-start | bytes 262144 | tf_op jit(solution)/shard_map/all_to_all | solution.py:171
  402.6 88.4 %all-gather.5.cloned.1.call-start = ((), (), s32[]{:S(2)}) async-start(), calls=%async_computation.5 | async-start | bytes 2162688 | tf_op jit(solution)/shard_map/all_gather | solution.py:107
  410.4 10.8 %slice-start = ((f32[256,768]{0,1:T(8,128)}), f32[256,512]{0,1:T(8,128)S(1)}, s32[]{:S(2)}) async-start(f32[256,768]{0,1:T(8,128)} %reduce-scatter.2.cloned.1.call-done), calls=%async_computation.6 | async-start | bytes 1048576 | tf_op jit(solution)/shard_map/slice | solution.py:91
  410.4 83.9 %all-to-all-start = ((bf16[32,256,128]{2,1,0:T(8,128)(2,1)}), bf16[32,256,128]{2,1,0:T(8,128)(2,1)}, u32[]{:S(2)}, u32[]{:S(2)}) async-start(bf16[32,256,128]{2,1,0:T(8,128)(2,1)} %stack.2), calls=%async_computation.1 | async-start | bytes 4194304 | tf_op jit(solution)/shard_map/all_to_all | solution.py:21
Sparse Core Ops, SparseCore 0:
  69.9 38.2 all-gather.2
  121.7 265.7 reduce-scatter.1
  405.9 85.0 all-gather.4
